TPU v7x, 32 devices: a whole 2x2x4 slice. The times are simulated.
32 devices in a mesh: groups: 1, rows: 32 (over z, y, x, core).
Axes of the slice: x: 2, y: 2, z: 4, core: 2. Of those that a mesh axis runs over, the one named last changes fastest.
Arguments:
- acts: bfloat16 [4096, 2, 4096], P(('groups', 'rows')), may hold values from -6 to 6
- grads_out: bfloat16 [4096, 2, 4096], P(('groups', 'rows')), may hold values from -6 to 6
- lengths: int32 [32], P('groups'), may hold values from 1 to 512, 4096 in all
- valid: int32 [4096], P(('groups', 'rows')), may hold values 0 or 1
- proj_in: bfloat16 [4096, 128], replicated, may hold values from -0.09375 to 0.09375
- proj_out: bfloat16 [4096, 128], replicated, may hold values from -0.09375 to 0.09375
- fisher_inv: float32 [2, 4096, 4096], P(None, 'rows'), may hold values from -1 to 2, as said below
- database: float32 [4096, 2, 4096], P(('groups', 'rows')), may hold values from -250 to 250
Outputs:
- zscores: float32 [32, 4096], P(None, ('groups', 'rows'))
Inputs may be any that keep to these rules, and one draw needn't show every extreme that they name: The lengths sum to 4096; the largest is exactly 512. `fisher_inv`: each of the 2 blocks is symmetric.
All inputs are finite; a program needn't handle non-finite values. No bound on the sum of `valid` on one device may be relied on, other than what follows from the above.
Results may differ from a plain program's by a relative error of at most 0.0042.
Values sent between devices are 32-bit elements; how exact they have to be, the bound alone decides.
No kernel may reach another device: no remote copies, remote signals or barrier semaphores. Data moves between devices by JAX's collectives and lax.ppermute only.
A program may use at most 64 MiB of HBM per device.

v0:
```python
import jax
import jax.numpy as jnp
from jax import lax
from jax.sharding import PartitionSpec as P


def shards(acts, grads_out, lengths, valid, proj_in, proj_out, fisher_inv, database):
    tok_rows = acts.shape[0]
    modules = acts.shape[1]
    proj_rank = proj_in.shape[1] // modules
    queries = lengths.shape[0]
    flat_width = proj_rank * proj_rank
    first_pos = lax.axis_index("rows") * tok_rows
    positions = first_pos + jnp.arange(tok_rows, dtype=jnp.int32)
    seg_ends = jnp.cumsum(lengths)
    segment = jnp.sum((seg_ends[None, :] <= positions[:, None]).astype(jnp.int32), axis=1)
    selector = (
        (segment[:, None] == jnp.arange(queries, dtype=jnp.int32)[None, :]) & (valid[:, None] == 1)
    ).astype(jnp.bfloat16)
    module_sums = []
    for m in range(modules):
        act_proj = jnp.dot(
            acts[:, m, :],
            proj_in[:, m * proj_rank : (m + 1) * proj_rank],
            preferred_element_type=jnp.float32,
        ).astype(jnp.bfloat16)
        grad_proj = jnp.dot(
            grads_out[:, m, :],
            proj_out[:, m * proj_rank : (m + 1) * proj_rank],
            preferred_element_type=jnp.float32,
        ).astype(jnp.bfloat16)
        spread = (selector[:, :, None] * grad_proj[:, None, :]).reshape(
            tok_rows, queries * proj_rank
        )
        module_sum = lax.dot_general(
            spread, act_proj, (((0,), (0,)), ((), ())), preferred_element_type=jnp.float32
        )
        module_sums.append(module_sum.reshape(queries, flat_width))
    partial_value = jnp.stack(module_sums, axis=1)
    summed = lax.psum(partial_value, "rows")
    precond_cols = jnp.einsum("qmk,mck->qmc", summed, fisher_inv, precision=lax.Precision.HIGHEST)
    scores = jnp.einsum(
        "qmk,nmk->qn",
        lax.all_gather(precond_cols, "rows", axis=2, tiled=True),
        database,
        precision=lax.Precision.HIGHEST,
    )
    db_count = database.shape[0] * lax.axis_size("rows")
    first_moment, second_moment = lax.psum(
        (jnp.sum(scores, axis=1), jnp.sum(scores * scores, axis=1)), "rows"
    )
    avg_score = first_moment / db_count
    variance = second_moment / db_count - avg_score * avg_score
    centred = scores - avg_score[:, None]
    return centred * lax.rsqrt(variance + 1e-06)[:, None]


def solution(mesh):
    placed = (
        P(("groups", "rows"), None, None),
        P(("groups", "rows"), None, None),
        P("groups"),
        P(("groups", "rows")),
        P(),
        P(),
        P(None, "rows", None),
        P(("groups", "rows"), None, None),
    )
    return jax.shard_map(
        shards, mesh=mesh, in_specs=placed, out_specs=P(None, ("groups", "rows")), check_vma=False
    )
```

profile of v0, /device:TPU:0, one launch (start us, length us, event | category | flops | bytes accessed | tf_op | source)
XLA Modules:
  0.0 286.0 jit_solution(3558763104719825832)
XLA Ops:
  6.5 6.1 %fusion.17 = (bf16[128,1,4096]{2,1,0:T(2,128)(2,1)S(1)}, bf16[128,1,4096]{2,1,0:T(2,128)(2,1)S(1)}) fusion(bf16[128,2,4096]{2,1,0:T(2,128)(2,1)} %param.9), kind=kLoop, calls=%fused_computation.33 | loop fusion | bytes 4194304 | tf_op jit(solution)/shard_map/slice | solution.py:28
  12.7 0.0 copy-start.3
  12.7 1.6 convolution_convert_fusion.1
  14.4 1.3 convolution_convert_fusion.3
  15.7 0.1 copy.21
  15.8 0.1 reduce-window.8
  15.8 0.1 reduce
  16.0 5.8 %fusion.16 = (bf16[128,1,4096]{2,1,0:T(2,128)(2,1)}, bf16[128,1,4096]{2,1,0:T(2,128)(2,1)}) fusion(bf16[128,2,4096]{2,1,0:T(2,128)(2,1)S(1)} %copy-done), kind=kLoop, calls=%fused_computation.32 | loop fusion | bytes 4194304 | tf_op jit(solution)/shard_map/slice | solution.py:23
  21.9 0.1 convert_reduce_fusion
  22.0 1.1 broadcast_multiply_fusion.1
  23.0 4.6 %fusion.2 = f32[2048,64]{1,0:T(8,128)} fusion(bf16[128,2048]{0,1:T(8,128)(2,1)} %bitcast.27, bf16[128,1,4096]{2,1,0:T(2,128)(2,1)} %get-tuple-element.9, bf16[4096,128]{1,0:T(8,128)(2,1)S(1)} %copy-done.2), kind=kOutput, calls=%fused_computation.7 | convolution fusion | flops 100671488 | bytes 3145728 | tf_op jit(solution)/shard_map/dot_general | solution.py:35
  27.6 2.4 stack_reshape.6
  30.0 4.0 %fusion.3 = f32[2048,64]{1,0:T(8,128)} fusion(bf16[128,2048]{0,1:T(8,128)(2,1)} %bitcast.26, bf16[128,1,4096]{2,1,0:T(2,128)(2,1)S(1)} %copy-done.1, bf16[4096,128]{1,0:T(8,128)(2,1)S(1)} %copy-done.2), kind=kOutput, calls=%fused_computation.8 | convolution fusion | flops 100671488 | bytes 3145728 | tf_op jit(solution)/shard_map/dot_general | solution.py:35
  34.0 1.6 stack_reshape.7
  35.6 2.1 pad_maximum_fusion
  37.7 0.0 all-reduce.3.cloned.1.call-update
  37.8 0.2 all-gather.2.cloned.1.call-start
  38.0 133.4 %all-reduce.3.cloned.1.call-done = f32[32,2,4096]{2,0,1:T(8,128)} async-done(((f32[32,2,4096]{2,0,1:T(8,128)}), f32[32,2,4096]{2,0,1:T(8,128)}) %all-reduce.3.cloned.1.call-update) | async-done | bytes 1048592 | tf_op jit(solution)/shard_map/psum | solution.py:40
  171.4 7.3 %convolution_bitcast_fusion = f32[32,2,128]{2,0,1:T(8,128)} fusion(f32[32,2,4096]{2,0,1:T(8,128)} %all-reduce.3.cloned.1.call-done, f32[2,128,4096]{2,1,0:T(8,128)} %param.14), kind=kOutput, calls=%fused_computation.2 | convolution fusion | flops 402653184 | bytes 5275648 | tf_op jit(solution)/shard_map/qmk,mck->qmc/dot_general | solution.py:41
  178.7 0.0 all-gather.2.cloned.1.call-update
  178.8 51.4 %all-gather.2.cloned.1.call-done = f32[32,2,4096]{2,0,1:T(8,128)} async-done(((f32[32,2,128]{2,0,1:T(8,128)}), f32[32,2,4096]{2,0,1:T(8,128)}) %all-gather.2.cloned.1.call-update) | async-done | bytes 1048592 | tf_op jit(solution)/shard_map/all_gather | solution.py:44
  230.2 8.2 %fusion.15 = (f32[32]{0:T(128)S(1)}, f32[32]{0:T(128)S(1)}, f32[32,128]{1,0:T(8,128)S(1)}) fusion(f32[32,2,4096]{2,0,1:T(8,128)} %all-gather.2.cloned.1.call-done, f32[128,2,4096]{2,1,0:T(2,128)} %param.15), kind=kOutput, calls=%fused_computation.31 | convolution fusion | flops 402665408 | bytes 5259520 | tf_op jit(solution)/shard_map/qmk,nmk->qn/dot_general | solution.py:42
  238.3 40.1 %all-reduce = (f32[32]{0:T(128)S(1)}, f32[32]{0:T(128)S(1)}) all-reduce(f32[32]{0:T(128)S(1)} %get-tuple-element.6, f32[32]{0:T(128)S(1)} %get-tuple-element.5), channel_id=1, replica_groups=mesh['groups'=1,'rows'=32] {'rows'}, use_global_device_ids=true, to_apply=%region_6.7 | all-reduce | flops 64 | bytes 512 | tf_op jit(solution)/shard_map/psum | solution.py:49
  278.5 0.7 subtract_multiply_fusion
  (16 shorter events, 0.1 us)
Async XLA Ops:
  6.5 164.9 %all-reduce.3.cloned.1.call-start = ((), (), s32[]{:S(2)}) async-start(), calls=%async_computation | async-start | bytes 2097152 | tf_op jit(solution)/shard_map/psum | solution.py:40
  6.5 6.1 %copy-start.4 = (bf16[4096,128]{1,0:T(8,128)(2,1)S(1)}, bf16[4096,128]{1,0:T(8,128)(2,1)}, u32[]{:S(2)}) copy-start(bf16[4096,128]{1,0:T(8,128)(2,1)} %param.13) | copy-start | bytes 3145732
  12.7 3.0 %copy-start.3 = (s32[32]{0:T(128)S(1)}, s32[32]{0:T(128)}, u32[]{:S(2)}) copy-start(s32[32]{0:T(128)} %param.10) | copy-start | bytes 388
  12.7 3.3 %copy-start.5 = (s32[128]{0:T(128)S(1)}, s32[128]{0:T(128)}, u32[]{:S(2)}) copy-start(s32[128]{0:T(128)} %param.11) | copy-start | bytes 1540
  12.7 3.3 %copy-start = (bf16[128,2,4096]{2,1,0:T(2,128)(2,1)S(1)}, bf16[128,2,4096]{2,1,0:T(2,128)(2,1)}, u32[]{:S(2)}) copy-start(bf16[128,2,4096]{2,1,0:T(2,128)(2,1)} %param.8) | copy-start | bytes 6291460
  16.0 7.0 %copy-start.2 = (bf16[4096,128]{1,0:T(8,128)(2,1)S(1)}, bf16[4096,128]{1,0:T(8,128)(2,1)}, u32[]{:S(2)}) copy-start(bf16[4096,128]{1,0:T(8,128)(2,1)} %param.12) | copy-start | bytes 3145732
  23.0 7.0 %copy-start.1 = (bf16[128,1,4096]{2,1,0:T(2,128)(2,1)S(1)}, bf16[128,1,4096]{2,1,0:T(2,128)(2,1)}, u32[]{:S(2)}) copy-start(bf16[128,1,4096]{2,1,0:T(2,128)(2,1)} %get-tuple-element.10) | copy-start | bytes 3145732
  37.8 192.4 %all-gather.2.cloned.1.call-start = ((), (), s32[]{:S(2)}) async-start(), calls=%async_computation.1 | async-start | bytes 1081344 | tf_op jit(solution)/shard_map/all_gather | solution.py:44
Sparse Core Ops, SparseCore 0:
  37.9 133.4 all-reduce.2
  178.9 51.2 all-gather.1
where the time goes:
time: 286 us
  waiting for transfers between devices  185 us (65%)
  blocking collectives  40.1 us (14%)
  matrix products  27.1 us (9%)
  local copies, waits for them, and re-layouts  16 us (6%)
  between operations  13.5 us (5%)
  other arithmetic  4.19 us (1%)
    psum x1, waiting for transfers between devices, shards(): summed = lax.psum(partial_value, 'rows')  133 us
    all_gather x1, waiting for transfers between devices, shards(): lax.all_gather(precond_cols, 'rows', axis=2, tiled=True)  51.4 us
    psum x1, blocking collectives, shards(): lax.psum((jnp.sum(scores, axis=1), jnp.sum(scores * scores, axis=1)), 'ro...  40.1 us
    dot_general x2, matrix products, shards(): lax.dot_general(spread, act_proj, (((0,), (0,)), ((), ())), preferred_ele...  8.6 us
    dot_general x1, matrix products, shards(): jnp.einsum('qmk,nmk->qn', lax.all_gather(precond_cols, 'rows', axis=2, ti...  8.16 us
    dot_general x1, matrix products, shards(): jnp.einsum('qmk,mck->qmc', summed, fisher_inv, precision=lax.Precision.HI...  7.35 us
    slice x1, local copies, waits for them, and re-layouts, shards(): grads_out[:, m, :]  6.11 us
    slice x1, local copies, waits for them, and re-layouts, shards(): acts[:, m, :]  5.84 us
  transfers between devices with their start and end apart: 2, of which 2 were waited for; matrix products, arithmetic and copies ran while one was open for 0% of the time, Pallas kernels for 0%

commit v1 on v0

--- a/solution.py
+++ b/solution.py
@@ -2,6 +2,14 @@
 import jax.numpy as jnp
 from jax import lax
 from jax.sharding import PartitionSpec as P
+
+
+def add_in_pairs(block, name):
+    peers, total = (lax.axis_size(name), block)
+    for far in [1 << k for k in range(peers.bit_length() - 1)]:
+        route = [(i, i ^ far) for i in range(peers)]
+        total = total + lax.ppermute(total, name, route)
+    return total
 
 
 def shards(acts, grads_out, lengths, valid, proj_in, proj_out, fisher_inv, database):
@@ -37,7 +45,7 @@
         )
         module_sums.append(module_sum.reshape(queries, flat_width))
     partial_value = jnp.stack(module_sums, axis=1)
-    summed = lax.psum(partial_value, "rows")
+    summed = add_in_pairs(partial_value, "rows")
     precond_cols = jnp.einsum("qmk,mck->qmc", summed, fisher_inv, precision=lax.Precision.HIGHEST)
     scores = jnp.einsum(
         "qmk,nmk->qn",

time: 286 us -> 278 us (0.972)
  waiting for transfers between devices: 185 us -> 168 us
  starting transfers between devices: 0.22 us -> 9.19 us
  matrix products: 27.1 us -> 24 us
  local copies, waits for them, and re-layouts: 16 us -> 19 us
    psum x1 -> x0, waiting for transfers between devices: 133 us -> none  [shards(): summed = lax.psum(partial_value, 'rows')]
    ppermute x0 -> x5, waiting for transfers between devices: none -> 115 us  [add_in_pairs(): total = total + lax.ppermute(total, name, route)]
    ppermute x0 -> x5, starting transfers between devices: none -> 9.19 us  [add_in_pairs(): total = total + lax.ppermute(total, name, route)]
  transfers between devices with their start and end apart: 2 -> 6, of which waited for: 2 -> 6; matrix products, arithmetic and copies ran while one was open for 0% -> 0% of each run, Pallas kernels for 0% -> 0%
where the time goes in v1:
time: 278 us; the launch traced here: 277 us
  waiting for transfers between devices  168 us (60%)
  blocking collectives  40.1 us (14%)
  matrix products  24 us (9%)
  local copies, waits for them, and re-layouts  19 us (7%)
  between operations  13.5 us (5%)
  starting transfers between devices  9.19 us (3%)
  other arithmetic  3.53 us (1%)
    ppermute x5, waiting for transfers between devices, add_in_pairs(): total = total + lax.ppermute(total, name, route)  115 us
    all_gather x1, waiting for transfers between devices, shards(): lax.all_gather(precond_cols, 'rows', axis=2, tiled=True)  53 us
    psum x1, blocking collectives, shards(): lax.psum((jnp.sum(scores, axis=1), jnp.sum(scores * scores, axis=1)), 'ro...  40.1 us
    ppermute x5, starting transfers between devices, add_in_pairs(): total = total + lax.ppermute(total, name, route)  9.19 us
    dot_general x2, matrix products, shards(): lax.dot_general(spread, act_proj, (((0,), (0,)), ((), ())), preferred_ele...  8.27 us
    dot_general x1, matrix products, shards(): jnp.einsum('qmk,nmk->qn', lax.all_gather(precond_cols, 'rows', axis=2, ti...  8.16 us
    slice x1, local copies, waits for them, and re-layouts, shards(): grads_out[:, m, :]  6.27 us
    slice x1, local copies, waits for them, and re-layouts, shards(): acts[:, m, :]  5.82 us
  transfers between devices with their start and end apart: 6, of which 6 were waited for; matrix products, arithmetic and copies ran while one was open for 0% of the time, Pallas kernels for 0%

profile of v1, /device:TPU:0, one launch (start us, length us, event | category | flops | bytes accessed | tf_op | source)
XLA Modules:
  0.0 277.5 jit_solution(10707932408609208104)
XLA Ops:
  6.5 6.3 %fusion.18 = (bf16[128,1,4096]{2,1,0:T(2,128)(2,1)S(1)}, bf16[128,1,4096]{2,1,0:T(2,128)(2,1)S(1)}) fusion(bf16[128,2,4096]{2,1,0:T(2,128)(2,1)} %param.9), kind=kLoop, calls=%fused_computation.35 | loop fusion | bytes 4194304 | tf_op jit(solution)/shard_map/slice | solution.py:36
  12.9 1.6 convolution_convert_fusion.1
  14.5 1.3 convolution_convert_fusion.3
  16.2 5.8 %fusion.17 = (bf16[128,1,4096]{2,1,0:T(2,128)(2,1)}, bf16[128,1,4096]{2,1,0:T(2,128)(2,1)}) fusion(bf16[128,2,4096]{2,1,0:T(2,128)(2,1)S(1)} %copy-done), kind=kLoop, calls=%fused_computation.34 | loop fusion | bytes 4194304 | tf_op jit(solution)/shard_map/slice | solution.py:31
  22.1 0.9 broadcast_multiply_fusion
  23.0 4.3 %fusion.2 = f32[2048,64]{1,0:T(8,128)} fusion(bf16[128,2048]{0,1:T(8,128)(2,1)S(1)} %bitcast.26, bf16[128,1,4096]{2,1,0:T(2,128)(2,1)} %get-tuple-element.10, bf16[4096,128]{1,0:T(8,128)(2,1)S(1)} %copy-done.2), kind=kOutput, calls=%fused_computation.7 | convolution fusion | flops 100671488 | bytes 3145728 | tf_op jit(solution)/shard_map/dot_general | solution.py:43
  27.3 2.5 stack_reshape.6
  29.8 1.9 constant_dynamic-update-slice_fusion.1
  31.7 4.0 %fusion.3 = f32[2048,64]{1,0:T(8,128)} fusion(bf16[128,2048]{0,1:T(8,128)(2,1)} %bitcast.25, bf16[128,1,4096]{2,1,0:T(2,128)(2,1)S(1)} %copy-done.1, bf16[4096,128]{1,0:T(8,128)(2,1)S(1)} %copy-done.2), kind=kOutput, calls=%fused_computation.8 | convolution fusion | flops 100671488 | bytes 3145728 | tf_op jit(solution)/shard_map/dot_general | solution.py:43
  35.7 1.6 stack_reshape.7
  38.6 2.5 collective-permute-done
  41.1 1.3 add.37
  42.4 2.9 %collective-permute-start.1 = (f32[32,2,4096]{2,0,1:T(8,128)S(1)}, f32[32,2,4096]{2,0,1:T(8,128)S(1)}, u32[]{:S(2)}, u32[]{:S(2)}) collective-permute-start(f32[32,2,4096]{2,0,1:T(8,128)S(1)} %add.37), channel_id=1, source_target_pairs={{0,2},{1,3},{2,0},{3,1},{4,6},{5,7},{6,4},{7,5},{8,10},{9,11},{10,... | collective-permute-start | bytes 3145736 | tf_op jit(solution)/shard_map/ppermute | solution.py:11
  45.3 23.5 %collective-permute-done.1 = f32[32,2,4096]{2,0,1:T(8,128)S(1)} collective-permute-done((f32[32,2,4096]{2,0,1:T(8,128)S(1)}, f32[32,2,4096]{2,0,1:T(8,128)S(1)}, u32[]{:S(2)}, u32[]{:S(2)}) %collective-permute-start.1) | collective-permute-done | bytes 1048608 | tf_op jit(solution)/shard_map/ppermute | solution.py:11
  68.9 1.8 collective-permute-start.2
  70.7 22.9 %collective-permute-done.2 = f32[32,2,4096]{2,0,1:T(8,128)S(1)} collective-permute-done((f32[32,2,4096]{2,0,1:T(8,128)S(1)}, f32[32,2,4096]{2,0,1:T(8,128)S(1)}, u32[]{:S(2)}, u32[]{:S(2)}) %collective-permute-start.2) | collective-permute-done | bytes 1048608 | tf_op jit(solution)/shard_map/ppermute | solution.py:11
  93.7 1.6 collective-permute-start.3
  95.3 22.2 %collective-permute-done.3 = f32[32,2,4096]{2,0,1:T(8,128)S(1)} collective-permute-done((f32[32,2,4096]{2,0,1:T(8,128)S(1)}, f32[32,2,4096]{2,0,1:T(8,128)S(1)}, u32[]{:S(2)}, u32[]{:S(2)}) %collective-permute-start.3) | collective-permute-done | bytes 1048608 | tf_op jit(solution)/shard_map/ppermute | solution.py:11
  117.7 2.3 collective-permute-start.4
  120.0 44.0 %collective-permute-done.4 = f32[32,2,4096]{2,0,1:T(8,128)S(1)} collective-permute-done((f32[32,2,4096]{2,0,1:T(8,128)S(1)}, f32[32,2,4096]{2,0,1:T(8,128)S(1)}, u32[]{:S(2)}, u32[]{:S(2)}) %collective-permute-start.4) | collective-permute-done | bytes 1048608 | tf_op jit(solution)/shard_map/ppermute | solution.py:11
  164.0 4.6 %convolution_bitcast_fusion = f32[32,2,128]{2,0,1:T(8,128)} fusion(f32[2,128,4096]{2,1,0:T(8,128)S(1)} %copy-done.3, f32[32,2,4096]{2,0,1:T(8,128)S(1)} %add.40, f32[32,2,4096]{2,0,1:T(8,128)S(1)} %collective-permute-done.4), kind=kOutput, calls=%fused_computation.2 | convolution fusion | flops 402915328 | bytes 6324224 | tf_op jit(solution)/shard_map/qmk,mck->qmc/dot_general | solution.py:49
  168.6 53.0 %all-gather.2.cloned.1.call-done = f32[32,2,4096]{2,0,1:T(8,128)} async-done(((f32[32,2,128]{2,0,1:T(8,128)}), f32[32,2,4096]{2,0,1:T(8,128)}) %all-gather.2.cloned.1.call-update) | async-done | bytes 1048592 | tf_op jit(solution)/shard_map/all_gather | solution.py:52
  221.6 8.2 %fusion.16 = (f32[32]{0:T(128)S(1)}, f32[32]{0:T(128)S(1)}, f32[32,128]{1,0:T(8,128)S(1)}) fusion(f32[32,2,4096]{2,0,1:T(8,128)} %all-gather.2.cloned.1.call-done, f32[128,2,4096]{2,1,0:T(2,128)} %param.15), kind=kOutput, calls=%fused_computation.33 | convolution fusion | flops 402665408 | bytes 5259520 | tf_op jit(solution)/shard_map/qmk,nmk->qn/dot_general | solution.py:50
  229.8 40.1 %all-reduce = (f32[32]{0:T(128)S(1)}, f32[32]{0:T(128)S(1)}) all-reduce(f32[32]{0:T(128)S(1)} %get-tuple-element.6, f32[32]{0:T(128)S(1)} %get-tuple-element.5), channel_id=1, replica_groups=mesh['groups'=1,'rows'=32] {'rows'}, use_global_device_ids=true, to_apply=%region_5.6 | all-reduce | flops 64 | bytes 512 | tf_op jit(solution)/shard_map/psum | solution.py:57
  (30 shorter events, 2.8 us)
Async XLA Ops:
  6.5 215.1 %all-gather.2.cloned.1.call-start = ((), (), s32[]{:S(2)}) async-start(), calls=%async_computation | async-start | bytes 1081344 | tf_op jit(solution)/shard_map/all_gather | solution.py:52
  6.5 6.3 %copy-start.5 = (bf16[4096,128]{1,0:T(8,128)(2,1)S(1)}, bf16[4096,128]{1,0:T(8,128)(2,1)}, u32[]{:S(2)}) copy-start(bf16[4096,128]{1,0:T(8,128)(2,1)} %param.13) | copy-start | bytes 3145732
  12.8 3.0 %copy-start.4 = (s32[32]{0:T(128)S(1)}, s32[32]{0:T(128)}, u32[]{:S(2)}) copy-start(s32[32]{0:T(128)} %param.10) | copy-start | bytes 388
  12.8 3.3 %copy-start.6 = (s32[128]{0:T(128)S(1)}, s32[128]{0:T(128)}, u32[]{:S(2)}) copy-start(s32[128]{0:T(128)} %param.11) | copy-start | bytes 1540
  12.9 3.3 %copy-start = (bf16[128,2,4096]{2,1,0:T(2,128)(2,1)S(1)}, bf16[128,2,4096]{2,1,0:T(2,128)(2,1)}, u32[]{:S(2)}) copy-start(bf16[128,2,4096]{2,1,0:T(2,128)(2,1)} %param.8) | copy-start | bytes 6291460
  16.2 6.8 %copy-start.2 = (bf16[4096,128]{1,0:T(8,128)(2,1)S(1)}, bf16[4096,128]{1,0:T(8,128)(2,1)}, u32[]{:S(2)}) copy-start(bf16[4096,128]{1,0:T(8,128)(2,1)} %param.12) | copy-start | bytes 3145732
  27.3 4.4 %copy-start.1 = (bf16[128,1,4096]{2,1,0:T(2,128)(2,1)S(1)}, bf16[128,1,4096]{2,1,0:T(2,128)(2,1)}, u32[]{:S(2)}) copy-start(bf16[128,1,4096]{2,1,0:T(2,128)(2,1)} %get-tuple-element.9) | copy-start | bytes 3145732
  38.1 3.0 %collective-permute-start = (f32[32,2,4096]{2,0,1:T(8,128)}, f32[32,2,4096]{2,0,1:T(8,128)S(1)}, u32[]{:S(2)}, u32[]{:S(2)}) collective-permute-start(f32[32,2,4096]{2,0,1:T(8,128)} %constant_dynamic-update-slice_fusion), channel_id=1, source_target_pairs={{0,1},{1,0},{2,3},{3,2},{4,5},{5,4},{6,7},{7,6},{8,9},{9,8},{10,11... | collective-permute-start | bytes 3145736 | tf_op jit(solution)/shard_map/ppermute | solution.py:11
  42.4 26.4 %collective-permute-start.1 = (f32[32,2,4096]{2,0,1:T(8,128)S(1)}, f32[32,2,4096]{2,0,1:T(8,128)S(1)}, u32[]{:S(2)}, u32[]{:S(2)}) collective-permute-start(f32[32,2,4096]{2,0,1:T(8,128)S(1)} %add.37), channel_id=1, source_target_pairs={{0,2},{1,3},{2,0},{3,1},{4,6},{5,7},{6,4},{7,5},{8,10},{9,11},{10,... | collective-permute-start | bytes 3145736 | tf_op jit(solution)/shard_map/ppermute | solution.py:11
  68.9 24.7 %collective-permute-start.2 = (f32[32,2,4096]{2,0,1:T(8,128)S(1)}, f32[32,2,4096]{2,0,1:T(8,128)S(1)}, u32[]{:S(2)}, u32[]{:S(2)}) collective-permute-start(f32[32,2,4096]{2,0,1:T(8,128)S(1)} %add.38), channel_id=1, source_target_pairs={{0,4},{1,5},{2,6},{3,7},{4,0},{5,1},{6,2},{7,3},{8,12},{9,13},{10,... | collective-permute-start | bytes 3145736 | tf_op jit(solution)/shard_map/ppermute | solution.py:11
  93.6 70.4 %copy-start.3 = (f32[2,128,4096]{2,1,0:T(8,128)S(1)}, f32[2,128,4096]{2,1,0:T(8,128)}, u32[]{:S(2)}) copy-start(f32[2,128,4096]{2,1,0:T(8,128)} %param.14) | copy-start | bytes 12582916
  93.7 23.8 %collective-permute-start.3 = (f32[32,2,4096]{2,0,1:T(8,128)S(1)}, f32[32,2,4096]{2,0,1:T(8,128)S(1)}, u32[]{:S(2)}, u32[]{:S(2)}) collective-permute-start(f32[32,2,4096]{2,0,1:T(8,128)S(1)} %add.39), channel_id=1, source_target_pairs={{0,8},{1,9},{2,10},{3,11},{4,12},{5,13},{6,14},{7,15},{8,0},{9,1},... | collective-permute-start | bytes 3145736 | tf_op jit(solution)/shard_map/ppermute | solution.py:11
  117.7 46.3 %collective-permute-start.4 = (f32[32,2,4096]{2,0,1:T(8,128)S(1)}, f32[32,2,4096]{2,0,1:T(8,128)S(1)}, u32[]{:S(2)}, u32[]{:S(2)}) collective-permute-start(f32[32,2,4096]{2,0,1:T(8,128)S(1)} %add.40), channel_id=1, source_target_pairs={{0,16},{1,17},{2,18},{3,19},{4,20},{5,21},{6,22},{7,23},{8,24},{9,... | collective-permute-start | bytes 3145736 | tf_op jit(solution)/shard_map/ppermute | solution.py:11
Sparse Core Ops, SparseCore 0:
  168.8 52.8 all-gather.1
